TPU v7x, 32 devices: a whole 2x2x4 slice. The times are simulated.
32 devices in a mesh: dp: 16 (over z, x, core), vocab: 2 (over y).
Axes of the slice: x: 2, y: 2, z: 4, core: 2. Of those that a mesh axis runs over, the one named last changes fastest.
Arguments:
- hidden: bfloat16 [2048, 8192], P('dp', 'vocab')
- rank_factor: bfloat16 [256, 8192], P(None, 'vocab'), may hold values from -0.0625 to 0.0625
- vocab_factor: bfloat16 [256, 77824], P('dp', 'vocab')
- lengths: int32 [2048], P('dp'), may hold values from 0 to 4096, as said below
- targets: int32 [2048], P('dp'), may hold values from 0 to 77823
- cotangent: bfloat16 [2048], P('dp'), may hold values from -96 to 96
- grammar: int32 [64, 22], P('dp', 'vocab'), may hold values from 0 to 1073741823, as said below
- assign: int32 [2048], P('dp'), may hold values from 0 to 127, as said below
Outputs:
- grad_hidden: bfloat16 [2048, 8192], P('dp', 'vocab')
- grad_factor: float32 [256, 8192], P('dp', 'vocab')
Inputs may be any that keep to these rules, and one draw needn't show every extreme that they name: `lengths`: in each aligned block of 128 rows the rows with a length above 0 come first; in every draw one such block has all 128 rows above 0 and a row of length 4096. `grammar`: only bits 0 to 29 of a word are used. `assign`: each aligned block of 128 entries is a permutation of 0 to 127.
All inputs are finite; a program needn't handle non-finite values.
Results may differ from a plain program's by a relative error of at most 0.0085.
Values may be sent and summed in bfloat16 or wider, within the bound.
No kernel may reach another device: no remote copies, remote signals or barrier semaphores. Data moves between devices by JAX's collectives and lax.ppermute only.
A program may use at most 128 MiB of HBM per device.

v0:
```python
import jax
import jax.numpy as jnp
from jax import lax
from jax.sharding import PartitionSpec as P

PREFIX_MAX = 4096
far_below = -1e30


def body(hidden, rank_factor, vocab_factor, lengths, targets, cotangent, grammar, assign):
    row_count = hidden.shape[0]
    rank = rank_factor.shape[0]
    groups = lax.axis_size("dp")
    share = row_count // groups
    width = vocab_factor.shape[1]
    tiles = width // 128
    first = lax.axis_index("vocab") * width
    factor = lax.all_gather(vocab_factor, "dp", axis=0, tiled=True)
    row_words = jnp.repeat(grammar, row_count // grammar.shape[0], axis=0)
    weight = cotangent.astype(jnp.float32) * lengths.astype(jnp.float32) / PREFIX_MAX
    partial_latent = lax.dot_general(
        hidden, rank_factor, (((1,), (1,)), ((), ())), preferred_element_type=jnp.float32
    )
    latent = lax.psum(partial_latent, "vocab").astype(jnp.bfloat16)
    target_local = targets - first
    columns = jnp.arange(width, dtype=jnp.int32)
    shifts = jnp.arange(30, dtype=jnp.int32)
    logits = jnp.dot(latent, factor, preferred_element_type=jnp.float32)
    bits = jnp.right_shift(row_words[:, :, None], shifts) & 1
    bits = bits.reshape(row_count, -1)[:, :tiles]
    tile_on = jnp.broadcast_to((bits == 1)[:, :, None], (row_count, tiles, 128)).reshape(
        row_count, width
    )
    target_hit = columns[None, :] == target_local[:, None]
    allowed = tile_on | target_hit
    masked = jnp.where(allowed, logits, far_below)
    peak = lax.pmax(jnp.max(masked, axis=1), "vocab")
    powers = jnp.where(allowed, jnp.exp(masked - peak[:, None]), 0.0)
    total = lax.psum(jnp.sum(powers, axis=1), "vocab")
    row_probs = powers / total[:, None]
    score_grad = (weight[:, None] * (row_probs - target_hit.astype(jnp.float32))).astype(
        jnp.bfloat16
    )
    rank_partial = lax.dot_general(
        score_grad, factor, (((1,), (1,)), ((), ())), preferred_element_type=jnp.float32
    )
    rank_grad = lax.psum(rank_partial, "vocab").astype(jnp.bfloat16)
    grad_factor = lax.psum_scatter(
        lax.dot_general(
            rank_grad, hidden, (((0,), (0,)), ((), ())), preferred_element_type=jnp.float32
        ).astype(jnp.bfloat16),
        "dp",
        scatter_dimension=0,
        tiled=True,
    ).astype(jnp.float32)
    picked = jnp.take(rank_grad, assign, axis=0).reshape(groups, share, rank)
    slot_rank = lax.all_to_all(picked, "dp", split_axis=0, concat_axis=0, tiled=True).reshape(
        row_count, rank
    )
    grad_hidden = jnp.dot(slot_rank, rank_factor, preferred_element_type=jnp.float32).astype(
        jnp.bfloat16
    )
    return (grad_hidden, grad_factor)


def solution(mesh):
    return jax.shard_map(
        body,
        mesh=mesh,
        in_specs=(
            P("dp", "vocab"),
            P(None, "vocab"),
            P("dp", "vocab"),
            P("dp"),
            P("dp"),
            P("dp"),
            P("dp", "vocab"),
            P("dp"),
        ),
        out_specs=(P("dp", "vocab"), P("dp", "vocab")),
        check_vma=False,
    )
```

profile of v0, /device:TPU:0, one launch (start us, length us, event | category | flops | bytes accessed | tf_op | source)
XLA Modules:
  0.0 263.4 jit_solution(1974408419297866180)
XLA Ops:
  7.2 0.0 copy-start
  7.2 0.0 all-gather.2.cloned.1.call-start
  7.2 0.7 all-gather.2.cloned.1.call-update
  7.9 0.0 reduce-scatter.2.cloned.1.call-start
  8.0 0.8 copy.10
  8.7 0.1 broadcast_in_dim.38
  8.8 0.1 shift_right_arithmetic.22
  9.0 0.1 shift_right_arithmetic.26
  9.0 0.1 fusion.4
  9.2 0.2 copy.11
  9.3 0.0 copy-done
  9.3 2.1 fusion.10
  11.4 11.4 %all-reduce.2 = bf16[128,256]{1,0:T(8,128)(2,1)S(1)} all-reduce(f32[128,256]{1,0:T(8,128)S(1)} %fusion.10), channel_id=1, replica_groups=mesh['dp'=16,'vocab'=2] {'vocab'}, use_global_device_ids=true, to_apply=%region_0.0 | all-reduce | flops 32768 | bytes 196608 | tf_op jit(solution)/shard_map/psum | solution.py:24
  22.9 0.7 broadcast_subtract_fusion
  23.5 0.7 multiply_multiply_fusion
  24.2 92.0 %all-gather.2.cloned.1.call-done = bf16[256,38912]{1,0:T(8,128)(2,1)} async-done(((bf16[16,38912]{1,0:T(8,128)(2,1)}), bf16[256,38912]{1,0:T(8,128)(2,1)}) %all-gather.2.cloned.1.call-update) | async-done | bytes 19922960 | tf_op jit(solution)/shard_map/all_gather | solution.py:18
  116.2 6.6 %broadcast_in_dim.39 = pred[128,304,128]{2,1,0:T(8,128)(4,1)S(1)} broadcast(pred[128,304]{1,0:T(8,128)(4,1)S(1)} %copy.11), dimensions={0,1} | broadcast | bytes 5019648 | tf_op jit(solution)/shard_map/broadcast_in_dim | solution.py:31
  122.9 0.0 copy-start.1
  122.9 18.3 %fusion.9 = (f32[128]{0:T(128)S(1)}, f32[128,38912]{1,0:T(8,128)}) fusion(bf16[128,256]{1,0:T(8,128)(2,1)S(1)} %all-reduce.2, bf16[256,38912]{1,0:T(8,128)(2,1)} %all-gather.2.cloned.1.call-done, s32[128]{0:T(128)S(1)} %broadcast_subtract_fusion, pred[16,8,304,128]{3,2,1,0:T(8,128)(4,1)S(1)} %bitcast.28), kind=kOutput, calls=%fused_computation.22 | convolution fusion | flops 2570059776 | bytes 44893184 | tf_op jit(solution)/shard_map/dot_general | solution.py:28
  141.2 0.0 copy-done.1
  141.2 4.9 %pmax.7 = f32[128]{0:T(128)S(1)} all-reduce(f32[128]{0:T(128)S(1)} %get-tuple-element.2), channel_id=1, replica_groups=mesh['dp'=16,'vocab'=2] {'vocab'}, use_global_device_ids=true, to_apply=%region_2.3 | all-reduce | flops 128 | bytes 1024 | tf_op jit(solution)/shard_map/pmax | solution.py:37
  146.1 12.7 %fusion.1 = f32[128]{0:T(128)S(1)} fusion(f32[128,38912]{1,0:T(8,128)} %get-tuple-element.3, f32[128]{0:T(128)S(1)} %pmax.7, s32[128]{0:T(128)S(1)} %broadcast_subtract_fusion, pred[16,8,304,128]{3,2,1,0:T(8,128)(4,1)} %bitcast.29), kind=kLoop, calls=%fused_computation.6 | loop fusion | flops 24903552 | bytes 24905216 | tf_op jit(solution)/shard_map/reduce_sum | solution.py:39
  158.9 4.9 %psum.22 = f32[128]{0:T(128)S(1)} all-reduce(f32[128]{0:T(128)S(1)} %fusion.1), channel_id=1, replica_groups=mesh['dp'=16,'vocab'=2] {'vocab'}, use_global_device_ids=true, to_apply=%region_4.5 | all-reduce | flops 128 | bytes 1024 | tf_op jit(solution)/shard_map/psum | solution.py:39
  163.8 0.0 copy-start.2
  163.8 0.0 copy-start.3
  163.8 17.9 %fusion.2 = f32[128,256]{1,0:T(8,128)S(1)} fusion(bf16[256,38912]{1,0:T(8,128)(2,1)} %all-gather.2.cloned.1.call-done, f32[128,38912]{1,0:T(8,128)} %get-tuple-element.3, f32[128]{0:T(128)S(1)} %psum.22, f32[128]{0:T(128)S(1)} %pmax.7, s32[128]{0:T(128)S(1)} %broadcast_subtract_fusion, f32[128]{0:T(128)S(1)} %multiply_multiply_fusion, ...), kind=kOutput, calls=%fused_computation.7 | convolution fusion | flops 2594963456 | bytes 44959744 | tf_op jit(solution)/shard_map/dot_general | solution.py:44
  181.8 9.7 %all-reduce.3 = bf16[128,256]{1,0:T(8,128)(2,1)S(1)} all-reduce(f32[128,256]{1,0:T(8,128)S(1)} %fusion.2), channel_id=1, replica_groups=mesh['dp'=16,'vocab'=2] {'vocab'}, use_global_device_ids=true, to_apply=%region_5.6 | all-reduce | flops 32768 | bytes 196608 | tf_op jit(solution)/shard_map/psum | solution.py:47
  191.5 0.0 copy-done.2
  191.5 2.1 convolution_convert_fusion
  193.6 0.0 reduce-scatter.2.cloned.1.call-update
  193.6 0.0 copy-done.3
  193.6 0.1 broadcast_in_dim.36
  193.7 0.8 gather_fusion
  194.6 0.1 bitcast_select_fusion
  194.7 11.4 %all_to_all.5 = bf16[16,8,256]{2,1,0:T(8,128)(2,1)S(1)} all-to-all(bf16[16,8,256]{2,1,0:T(8,128)(2,1)S(1)} %bitcast_select_fusion), channel_id=1, replica_groups=mesh['dp'=16,'vocab'=2] {'dp'}, dimensions={0} | all-to-all | bytes 131072 | tf_op jit(solution)/shard_map/all_to_all | solution.py:57
  206.1 1.4 convolution_convert_fusion.1
  207.5 47.4 %reduce-scatter.2.cloned.1.call-done = bf16[16,4096]{1,0:T(8,128)(2,1)} async-done(((bf16[256,4096]{1,0:T(8,128)(2,1)}), bf16[16,4096]{1,0:T(8,128)(2,1)}) %reduce-scatter.2.cloned.1.call-update) | async-done | bytes 131088 | tf_op jit(solution)/shard_map/reduce_scatter | solution.py:48
  254.9 1.6 convert_element_type.35
  (6 shorter events, 0.1 us)
Async XLA Ops:
  7.2 2.2 copy-start
  7.2 109.1 %all-gather.2.cloned.1.call-start = ((), (), s32[]{:S(2)}) async-start(), calls=%async_computation.2 | async-start | bytes 21168128 | tf_op jit(solution)/shard_map/all_gather | solution.py:18
  7.9 247.0 %reduce-scatter.2.cloned.1.call-start = ((), (), s32[]{:S(2)}) async-start(), calls=%async_computation.3 | async-start | bytes 2228224 | tf_op jit(solution)/shard_map/reduce_scatter | solution.py:48
  122.9 18.3 %copy-start.1 = (pred[128,304,128]{2,1,0:T(8,128)(4,1)}, pred[128,304,128]{2,1,0:T(8,128)(4,1)S(1)}, u32[]{:S(2)}) copy-start(pred[128,304,128]{2,1,0:T(8,128)(4,1)S(1)} %broadcast_in_dim.39) | copy-start | bytes 14942212
  163.8 27.7 %copy-start.2 = (bf16[128,4096]{1,0:T(8,128)(2,1)S(1)}, bf16[128,4096]{1,0:T(8,128)(2,1)}, u32[]{:S(2)}) copy-start(bf16[128,4096]{1,0:T(8,128)(2,1)} %param.8) | copy-start | bytes 3145732
  163.8 29.8 %copy-start.3 = (s32[128]{0:T(128)S(1)}, s32[128]{0:T(128)}, u32[]{:S(2)}) copy-start(s32[128]{0:T(128)} %param.15) | copy-start | bytes 1540
Sparse Core Ops, SparseCore 0:
  9.6 106.5 all-gather.1
  193.7 61.1 reduce-scatter.1
where the time goes:
time: 264 us; the launch traced here: 263 us
  waiting for transfers between devices  140 us (53%)
  blocking collectives  42.4 us (16%)
  matrix products  41.8 us (16%)
  other arithmetic  15.9 us (6%)
  between operations  14.2 us (5%)
  local copies, waits for them, and re-layouts  8.79 us (3%)
    all_gather x1, waiting for transfers between devices, body(): factor = lax.all_gather(vocab_factor, 'dp', axis=0, tiled=True)  92 us
    reduce_scatter x1, waiting for transfers between devices, body(): lax.psum_scatter(lax.dot_general(rank_grad, hidden, (((0,), (0,)), ((), (...  47.4 us
    dot_general x1, matrix products, body(): logits = jnp.dot(latent, factor, preferred_element_type=jnp.float32)  18.3 us
    dot_general x1, matrix products, body(): lax.dot_general(score_grad, factor, (((1,), (1,)), ((), ())), preferred_e...  17.9 us
    reduce_sum x1, other arithmetic, body(): total = lax.psum(jnp.sum(powers, axis=1), 'vocab')  12.7 us
    psum x1, blocking collectives, body(): latent = lax.psum(partial_latent, 'vocab').astype(jnp.bfloat16)  11.4 us
    all_to_all x1, blocking collectives, body(): lax.all_to_all(picked, 'dp', split_axis=0, concat_axis=0, tiled=True)  11.4 us
    psum x1, blocking collectives, body(): rank_grad = lax.psum(rank_partial, 'vocab').astype(jnp.bfloat16)  9.72 us
  transfers between devices with their start and end apart: 2, of which 2 were waited for; matrix products, arithmetic and copies ran while one was open for 3% of the time, Pallas kernels for 0%

commit v1 on v0

--- a/solution.py
+++ b/solution.py
@@ -15,7 +15,12 @@
     width = vocab_factor.shape[1]
     tiles = width // 128
     first = lax.axis_index("vocab") * width
-    factor = lax.all_gather(vocab_factor, "dp", axis=0, tiled=True)
+    ring = [vocab_factor]
+    for hop in range(15):
+        ring.append(lax.ppermute(ring[-1], "dp", [(dev, (dev + 1) % 16) for dev in range(16)]))
+    factor = jnp.roll(
+        jnp.concatenate(ring[::-1], axis=0), (lax.axis_index("dp") + 1) * ring[0].shape[0], axis=0
+    )
     row_words = jnp.repeat(grammar, row_count // grammar.shape[0], axis=0)
     weight = cotangent.astype(jnp.float32) * lengths.astype(jnp.float32) / PREFIX_MAX
     partial_latent = lax.dot_general(

time: 264 us -> 503 us (1.91)
  waiting for transfers between devices: 140 us -> 316 us
  local copies, waits for them, and re-layouts: 8.79 us -> 73.3 us
    ppermute x0 -> x15, waiting for transfers between devices: none -> 270 us  [body(): lax.ppermute(ring[-1], 'dp', [(dev, (dev + 1) % 16) for dev in range(16)])]
    all_gather x1 -> x0, waiting for transfers between devices: 92 us -> none  [body(): factor = lax.all_gather(vocab_factor, 'dp', axis=0, tiled=True)]
    unnamed x9 -> x94, local copies, waits for them, and re-layouts: 0.79 us -> 63.4 us
  transfers between devices with their start and end apart: 2 -> 16, of which waited for: 2 -> 16; matrix products, arithmetic and copies ran while one was open for 3% -> 2% of each run, Pallas kernels for 0% -> 0%
where the time goes in v1:
time: 503 us
  waiting for transfers between devices  316 us (63%)
  local copies, waits for them, and re-layouts  73.3 us (15%)
  matrix products  41.6 us (8%)
  blocking collectives  40.5 us (8%)
  other arithmetic  16.5 us (3%)
  between operations  14.3 us (3%)
    ppermute x15, waiting for transfers between devices, body(): lax.ppermute(ring[-1], 'dp', [(dev, (dev + 1) % 16) for dev in range(16)])  270 us
    unnamed x94, local copies, waits for them, and re-layouts  63.4 us
    reduce_scatter x1, waiting for transfers between devices, body(): lax.psum_scatter(lax.dot_general(rank_grad, hidden, (((0,), (0,)), ((), (...  45.6 us
    dot_general x1, matrix products, body(): lax.dot_general(score_grad, factor, (((1,), (1,)), ((), ())), preferred_e...  18 us
    dot_general x1, matrix products, body(): logits = jnp.dot(latent, factor, preferred_element_type=jnp.float32)  18 us
    reduce_sum x1, other arithmetic, body(): total = lax.psum(jnp.sum(powers, axis=1), 'vocab')  12.7 us
    psum x1, blocking collectives, body(): latent = lax.psum(partial_latent, 'vocab').astype(jnp.bfloat16)  10.7 us
    psum x1, blocking collectives, body(): rank_grad = lax.psum(rank_partial, 'vocab').astype(jnp.bfloat16)  10.2 us
  transfers between devices with their start and end apart: 16, of which 16 were waited for; matrix products, arithmetic and copies ran while one was open for 2% of the time, Pallas kernels for 0%

profile of v1, /device:TPU:0, one launch (start us, length us, event | category | flops | bytes accessed | tf_op | source)
XLA Modules:
  0.0 502.6 jit_solution(8616262611723640237)
XLA Ops:
  7.7 19.8 %collective-permute-done = bf16[16,38912]{1,0:T(8,128)(2,1)S(1)} collective-permute-done((bf16[16,38912]{1,0:T(8,128)(2,1)}, bf16[16,38912]{1,0:T(8,128)(2,1)S(1)}, u32[]{:S(2)}, u32[]{:S(2)}) %collective-permute-start) | collective-permute-done | bytes 1245216 | tf_op jit(solution)/shard_map/ppermute | solution.py:20
  28.6 19.0 %collective-permute-done.1 = bf16[16,38912]{1,0:T(8,128)(2,1)S(1)} collective-permute-done((bf16[16,38912]{1,0:T(8,128)(2,1)S(1)}, bf16[16,38912]{1,0:T(8,128)(2,1)S(1)}, u32[]{:S(2)}, u32[]{:S(2)}) %collective-permute-start.1) | collective-permute-done | bytes 1245216 | tf_op jit(solution)/shard_map/ppermute | solution.py:20
  48.6 19.0 %collective-permute-done.2 = bf16[16,38912]{1,0:T(8,128)(2,1)S(1)} collective-permute-done((bf16[16,38912]{1,0:T(8,128)(2,1)S(1)}, bf16[16,38912]{1,0:T(8,128)(2,1)S(1)}, u32[]{:S(2)}, u32[]{:S(2)}) %collective-permute-start.2) | collective-permute-done | bytes 1245216 | tf_op jit(solution)/shard_map/ppermute | solution.py:20
  68.7 19.0 %collective-permute-done.3 = bf16[16,38912]{1,0:T(8,128)(2,1)S(1)} collective-permute-done((bf16[16,38912]{1,0:T(8,128)(2,1)S(1)}, bf16[16,38912]{1,0:T(8,128)(2,1)S(1)}, u32[]{:S(2)}, u32[]{:S(2)}) %collective-permute-start.3) | collective-permute-done | bytes 1245216 | tf_op jit(solution)/shard_map/ppermute | solution.py:20
  88.8 19.0 %collective-permute-done.4 = bf16[16,38912]{1,0:T(8,128)(2,1)S(1)} collective-permute-done((bf16[16,38912]{1,0:T(8,128)(2,1)S(1)}, bf16[16,38912]{1,0:T(8,128)(2,1)S(1)}, u32[]{:S(2)}, u32[]{:S(2)}) %collective-permute-start.4) | collective-permute-done | bytes 1245216 | tf_op jit(solution)/shard_map/ppermute | solution.py:20
  108.9 19.0 %collective-permute-done.5 = bf16[16,38912]{1,0:T(8,128)(2,1)S(1)} collective-permute-done((bf16[16,38912]{1,0:T(8,128)(2,1)S(1)}, bf16[16,38912]{1,0:T(8,128)(2,1)S(1)}, u32[]{:S(2)}, u32[]{:S(2)}) %collective-permute-start.5) | collective-permute-done | bytes 1245216 | tf_op jit(solution)/shard_map/ppermute | solution.py:20
  129.0 19.0 %collective-permute-done.6 = bf16[16,38912]{1,0:T(8,128)(2,1)S(1)} collective-permute-done((bf16[16,38912]{1,0:T(8,128)(2,1)S(1)}, bf16[16,38912]{1,0:T(8,128)(2,1)S(1)}, u32[]{:S(2)}, u32[]{:S(2)}) %collective-permute-start.6) | collective-permute-done | bytes 1245216 | tf_op jit(solution)/shard_map/ppermute | solution.py:20
  148.0 1.1 copy-done.14
  149.1 19.0 %collective-permute-done.7 = bf16[16,38912]{1,0:T(8,128)(2,1)S(1)} collective-permute-done((bf16[16,38912]{1,0:T(8,128)(2,1)S(1)}, bf16[16,38912]{1,0:T(8,128)(2,1)S(1)}, u32[]{:S(2)}, u32[]{:S(2)}) %collective-permute-start.7) | collective-permute-done | bytes 1245216 | tf_op jit(solution)/shard_map/ppermute | solution.py:20
  169.1 19.0 %collective-permute-done.8 = bf16[16,38912]{1,0:T(8,128)(2,1)S(1)} collective-permute-done((bf16[16,38912]{1,0:T(8,128)(2,1)S(1)}, bf16[16,38912]{1,0:T(8,128)(2,1)S(1)}, u32[]{:S(2)}, u32[]{:S(2)}) %collective-permute-start.8) | collective-permute-done | bytes 1245216 | tf_op jit(solution)/shard_map/ppermute | solution.py:20
  189.2 19.0 %collective-permute-done.9 = bf16[16,38912]{1,0:T(8,128)(2,1)S(1)} collective-permute-done((bf16[16,38912]{1,0:T(8,128)(2,1)S(1)}, bf16[16,38912]{1,0:T(8,128)(2,1)S(1)}, u32[]{:S(2)}, u32[]{:S(2)}) %collective-permute-start.9) | collective-permute-done | bytes 1245216 | tf_op jit(solution)/shard_map/ppermute | solution.py:20
  208.3 1.1 copy-done.20
  209.3 19.0 %collective-permute-done.10 = bf16[16,38912]{1,0:T(8,128)(2,1)S(1)} collective-permute-done((bf16[16,38912]{1,0:T(8,128)(2,1)S(1)}, bf16[16,38912]{1,0:T(8,128)(2,1)S(1)}, u32[]{:S(2)}, u32[]{:S(2)}) %collective-permute-start.10) | collective-permute-done | bytes 1245216 | tf_op jit(solution)/shard_map/ppermute | solution.py:20
  229.4 19.0 %collective-permute-done.11 = bf16[16,38912]{1,0:T(8,128)(2,1)S(1)} collective-permute-done((bf16[16,38912]{1,0:T(8,128)(2,1)S(1)}, bf16[16,38912]{1,0:T(8,128)(2,1)S(1)}, u32[]{:S(2)}, u32[]{:S(2)}) %collective-permute-start.11) | collective-permute-done | bytes 1245216 | tf_op jit(solution)/shard_map/ppermute | solution.py:20
  249.5 19.0 %collective-permute-done.12 = bf16[16,38912]{1,0:T(8,128)(2,1)S(1)} collective-permute-done((bf16[16,38912]{1,0:T(8,128)(2,1)S(1)}, bf16[16,38912]{1,0:T(8,128)(2,1)S(1)}, u32[]{:S(2)}, u32[]{:S(2)}) %collective-permute-start.12) | collective-permute-done | bytes 1245216 | tf_op jit(solution)/shard_map/ppermute | solution.py:20
  269.5 19.1 %collective-permute-done.13 = bf16[16,38912]{1,0:T(8,128)(2,1)} collective-permute-done((bf16[16,38912]{1,0:T(8,128)(2,1)S(1)}, bf16[16,38912]{1,0:T(8,128)(2,1)}, u32[]{:S(2)}, u32[]{:S(2)}) %collective-permute-start.13) | collective-permute-done | bytes 1245216 | tf_op jit(solution)/shard_map/ppermute | solution.py:20
  290.0 2.2 fusion.14
  292.2 10.7 %all-reduce.2 = bf16[128,256]{1,0:T(8,128)(2,1)} all-reduce(f32[128,256]{1,0:T(8,128)S(1)} %fusion.14), channel_id=1, replica_groups=mesh['dp'=16,'vocab'=2] {'vocab'}, use_global_device_ids=true, to_apply=%region_0.1 | all-reduce | flops 32768 | bytes 196608 | tf_op jit(solution)/shard_map/psum | solution.py:29
  303.8 1.1 multiply_multiply_fusion
  304.9 3.1 collective-permute-done.14
  308.0 2.4 constant_dynamic-update-slice_fusion.31
  310.4 2.4 constant_dynamic-update-slice_fusion.30
  312.8 2.5 constant_dynamic-update-slice_fusion.29
  315.3 2.5 constant_dynamic-update-slice_fusion.28
  317.9 2.6 constant_dynamic-update-slice_fusion.27
  320.4 2.5 constant_dynamic-update-slice_fusion.26
  322.9 2.6 constant_dynamic-update-slice_fusion.25
  325.5 2.5 constant_dynamic-update-slice_fusion.24
  328.0 1.1 constant_dynamic-update-slice_fusion.23
  329.1 1.1 constant_dynamic-update-slice_fusion.22
  330.3 1.2 constant_dynamic-update-slice_fusion.21
  331.5 1.1 constant_dynamic-update-slice_fusion.20
  332.6 1.2 constant_dynamic-update-slice_fusion.19
  333.7 1.1 constant_dynamic-update-slice_fusion.18
  334.8 1.2 constant_dynamic-update-slice_fusion.17
  336.0 1.1 constant_dynamic-update-slice_fusion.16
  337.1 2.4 constant_dynamic-update-slice_fusion.15
  339.6 2.5 constant_dynamic-update-slice_fusion.14
  342.0 1.2 constant_dynamic-update-slice_fusion.13
  343.2 1.2 constant_dynamic-update-slice_fusion.12
  344.4 1.2 constant_dynamic-update-slice_fusion.11
  345.6 1.1 constant_dynamic-update-slice_fusion.10
  346.7 1.1 constant_dynamic-update-slice_fusion.9
  347.9 1.2 constant_dynamic-update-slice_fusion.8
  349.0 1.1 constant_dynamic-update-slice_fusion.7
  350.2 1.1 constant_dynamic-update-slice_fusion.6
  351.3 1.1 constant_dynamic-update-slice_fusion.5
  352.4 1.1 constant_dynamic-update-slice_fusion.4
  353.6 1.1 constant_dynamic-update-slice_fusion.3
  354.7 1.2 constant_dynamic-update-slice_fusion.2
  355.8 1.1 constant_dynamic-update-slice_fusion.1
  357.0 1.1 constant_dynamic-update-slice_fusion
  358.1 7.4 %broadcast_in_dim.39 = pred[128,304,128]{2,1,0:T(8,128)(4,1)} broadcast(pred[128,304]{1,0:T(8,128)(4,1)S(1)} %copy.11), dimensions={0,1} | broadcast | bytes 5019648 | tf_op jit(solution)/shard_map/broadcast_in_dim | solution.py:36
  365.5 18.0 %fusion.13 = (f32[128]{0:T(128)S(1)}, f32[128,38912]{1,0:T(8,128)}) fusion(bf16[128,256]{1,0:T(8,128)(2,1)S(1)} %copy-done.29, bf16[512,38912]{1,0:T(8,128)(2,1)} %constant_dynamic-update-slice_fusion, s32[]{:T(128)S(6)} %select_n.32, s32[128]{0:T(128)S(1)} %broadcast_subtract_fusion, pred[16,8,304,128]{3,2,1,0:T(8,128)(4,1)} %bitcast.26), kind=kOutput, calls=%fused_computation.58 | convolution fusion | flops 2570059776 | bytes 44893188 | tf_op jit(solution)/shard_map/dot_general | solution.py:33
  383.4 5.1 %pmax.7 = f32[128]{0:T(128)S(1)} all-reduce(f32[128]{0:T(128)S(1)} %get-tuple-element.2), channel_id=1, replica_groups=mesh['dp'=16,'vocab'=2] {'vocab'}, use_global_device_ids=true, to_apply=%region_2.3 | all-reduce | flops 128 | bytes 1024 | tf_op jit(solution)/shard_map/pmax | solution.py:42
  388.5 12.7 %fusion.4 = f32[128]{0:T(128)S(1)} fusion(f32[128,38912]{1,0:T(8,128)} %get-tuple-element.3, f32[128]{0:T(128)S(1)} %pmax.7, s32[128]{0:T(128)S(1)} %broadcast_subtract_fusion, pred[16,8,304,128]{3,2,1,0:T(8,128)(4,1)} %bitcast.27), kind=kLoop, calls=%fused_computation.9 | loop fusion | flops 24903552 | bytes 24905216 | tf_op jit(solution)/shard_map/reduce_sum | solution.py:44
  401.3 4.9 psum.22
  406.2 18.0 %fusion.1 = f32[128,256]{1,0:T(8,128)S(1)} fusion(bf16[512,38912]{1,0:T(8,128)(2,1)} %constant_dynamic-update-slice_fusion, s32[]{:T(128)S(6)} %select_n.32, f32[128,38912]{1,0:T(8,128)} %get-tuple-element.3, f32[128]{0:T(128)S(1)} %psum.22, f32[128]{0:T(128)S(1)} %pmax.7, s32[128]{0:T(128)S(1)} %broadcast_subtract_fusion, ...), kind=kOutput, calls=%fused_computation.6 | convolution fusion | flops 2594963456 | bytes 44959748 | tf_op jit(solution)/shard_map/dot_general | solution.py:49
  424.2 10.2 %all-reduce.3 = bf16[128,256]{1,0:T(8,128)(2,1)S(1)} all-reduce(f32[128,256]{1,0:T(8,128)S(1)} %fusion.1), channel_id=1, replica_groups=mesh['dp'=16,'vocab'=2] {'vocab'}, use_global_device_ids=true, to_apply=%region_5.6 | all-reduce | flops 32768 | bytes 196608 | tf_op jit(solution)/shard_map/psum | solution.py:52
  434.5 2.1 convolution_convert_fusion
  437.6 9.5 %all_to_all.5 = bf16[16,8,256]{2,1,0:T(8,128)(2,1)S(1)} all-to-all(bf16[16,8,256]{2,1,0:T(8,128)(2,1)S(1)} %bitcast_select_fusion), channel_id=1, replica_groups=mesh['dp'=16,'vocab'=2] {'dp'}, dimensions={0} | all-to-all | bytes 131072 | tf_op jit(solution)/shard_map/all_to_all | solution.py:62
  447.1 1.4 convolution_convert_fusion.1
  448.5 45.6 %reduce-scatter.2.cloned.1.call-done = bf16[16,4096]{1,0:T(8,128)(2,1)} async-done(((bf16[256,4096]{1,0:T(8,128)(2,1)}), bf16[16,4096]{1,0:T(8,128)(2,1)}) %reduce-scatter.2.cloned.1.call-update) | async-done | bytes 131088 | tf_op jit(solution)/shard_map/reduce_scatter | solution.py:53
  494.2 1.6 convert_element_type.35
  (93 shorter events, 15.3 us)
Async XLA Ops:
  7.2 282.8 %copy-start = (bf16[256,4096]{1,0:T(8,128)(2,1)S(1)}, bf16[256,4096]{1,0:T(8,128)(2,1)}, u32[]{:S(2)}) copy-start(bf16[256,4096]{1,0:T(8,128)(2,1)} %param.9) | copy-start | bytes 6291460
  7.2 487.0 %reduce-scatter.2.cloned.1.call-start = ((), (), s32[]{:S(2)}) async-start(), calls=%async_computation.2 | async-start | bytes 2228224 | tf_op jit(solution)/shard_map/reduce_scatter | solution.py:53
  7.2 20.3 %collective-permute-start = (bf16[16,38912]{1,0:T(8,128)(2,1)}, bf16[16,38912]{1,0:T(8,128)(2,1)S(1)}, u32[]{:S(2)}, u32[]{:S(2)}) collective-permute-start(bf16[16,38912]{1,0:T(8,128)(2,1)} %param.10), channel_id=1, source_target_pairs={{0,2},{2,4},{4,6},{6,8},{8,10},{10,12},{12,14},{14,16},{16,18},{18... | collective-permute-start | bytes 3735560 | tf_op jit(solution)/shard_map/ppermute | solution.py:20
  27.5 1.1 copy-start.2
  28.6 19.0 %collective-permute-start.1 = (bf16[16,38912]{1,0:T(8,128)(2,1)S(1)}, bf16[16,38912]{1,0:T(8,128)(2,1)S(1)}, u32[]{:S(2)}, u32[]{:S(2)}) collective-permute-start(bf16[16,38912]{1,0:T(8,128)(2,1)S(1)} %collective-permute-done), channel_id=1, source_target_pairs={{0,2},{2,4},{4,6},{6,8},{8,10},{10,12},{12,14},{14,16},{16,18},{18... | collective-permute-start | bytes 3735560 | tf_op jit(solution)/shard_map/ppermute | solution.py:20
  47.6 1.0 copy-start.4
  48.6 19.0 %collective-permute-start.2 = (bf16[16,38912]{1,0:T(8,128)(2,1)S(1)}, bf16[16,38912]{1,0:T(8,128)(2,1)S(1)}, u32[]{:S(2)}, u32[]{:S(2)}) collective-permute-start(bf16[16,38912]{1,0:T(8,128)(2,1)S(1)} %collective-permute-done.1), channel_id=1, source_target_pairs={{0,2},{2,4},{4,6},{6,8},{8,10},{10,12},{12,14},{14,16},{16,18},{18... | collective-permute-start | bytes 3735560 | tf_op jit(solution)/shard_map/ppermute | solution.py:20
  67.7 1.0 copy-start.6
  68.7 19.0 %collective-permute-start.3 = (bf16[16,38912]{1,0:T(8,128)(2,1)S(1)}, bf16[16,38912]{1,0:T(8,128)(2,1)S(1)}, u32[]{:S(2)}, u32[]{:S(2)}) collective-permute-start(bf16[16,38912]{1,0:T(8,128)(2,1)S(1)} %collective-permute-done.2), channel_id=1, source_target_pairs={{0,2},{2,4},{4,6},{6,8},{8,10},{10,12},{12,14},{14,16},{16,18},{18... | collective-permute-start | bytes 3735560 | tf_op jit(solution)/shard_map/ppermute | solution.py:20
  87.7 1.0 copy-start.8
  88.8 19.0 %collective-permute-start.4 = (bf16[16,38912]{1,0:T(8,128)(2,1)S(1)}, bf16[16,38912]{1,0:T(8,128)(2,1)S(1)}, u32[]{:S(2)}, u32[]{:S(2)}) collective-permute-start(bf16[16,38912]{1,0:T(8,128)(2,1)S(1)} %collective-permute-done.3), channel_id=1, source_target_pairs={{0,2},{2,4},{4,6},{6,8},{8,10},{10,12},{12,14},{14,16},{16,18},{18... | collective-permute-start | bytes 3735560 | tf_op jit(solution)/shard_map/ppermute | solution.py:20
  107.8 1.1 copy-start.10
  108.9 19.0 %collective-permute-start.5 = (bf16[16,38912]{1,0:T(8,128)(2,1)S(1)}, bf16[16,38912]{1,0:T(8,128)(2,1)S(1)}, u32[]{:S(2)}, u32[]{:S(2)}) collective-permute-start(bf16[16,38912]{1,0:T(8,128)(2,1)S(1)} %collective-permute-done.4), channel_id=1, source_target_pairs={{0,2},{2,4},{4,6},{6,8},{8,10},{10,12},{12,14},{14,16},{16,18},{18... | collective-permute-start | bytes 3735560 | tf_op jit(solution)/shard_map/ppermute | solution.py:20
  127.9 1.1 copy-start.12
  128.9 19.0 %collective-permute-start.6 = (bf16[16,38912]{1,0:T(8,128)(2,1)S(1)}, bf16[16,38912]{1,0:T(8,128)(2,1)S(1)}, u32[]{:S(2)}, u32[]{:S(2)}) collective-permute-start(bf16[16,38912]{1,0:T(8,128)(2,1)S(1)} %collective-permute-done.5), channel_id=1, source_target_pairs={{0,2},{2,4},{4,6},{6,8},{8,10},{10,12},{12,14},{14,16},{16,18},{18... | collective-permute-start | bytes 3735560 | tf_op jit(solution)/shard_map/ppermute | solution.py:20
  148.0 1.1 copy-start.14
  149.1 19.0 %collective-permute-start.7 = (bf16[16,38912]{1,0:T(8,128)(2,1)S(1)}, bf16[16,38912]{1,0:T(8,128)(2,1)S(1)}, u32[]{:S(2)}, u32[]{:S(2)}) collective-permute-start(bf16[16,38912]{1,0:T(8,128)(2,1)S(1)} %collective-permute-done.6), channel_id=1, source_target_pairs={{0,2},{2,4},{4,6},{6,8},{8,10},{10,12},{12,14},{14,16},{16,18},{18... | collective-permute-start | bytes 3735560 | tf_op jit(solution)/shard_map/ppermute | solution.py:20
  168.1 1.0 copy-start.16
  169.1 19.0 %collective-permute-start.8 = (bf16[16,38912]{1,0:T(8,128)(2,1)S(1)}, bf16[16,38912]{1,0:T(8,128)(2,1)S(1)}, u32[]{:S(2)}, u32[]{:S(2)}) collective-permute-start(bf16[16,38912]{1,0:T(8,128)(2,1)S(1)} %collective-permute-done.7), channel_id=1, source_target_pairs={{0,2},{2,4},{4,6},{6,8},{8,10},{10,12},{12,14},{14,16},{16,18},{18... | collective-permute-start | bytes 3735560 | tf_op jit(solution)/shard_map/ppermute | solution.py:20
  188.2 1.1 copy-start.18
  189.2 19.0 %collective-permute-start.9 = (bf16[16,38912]{1,0:T(8,128)(2,1)S(1)}, bf16[16,38912]{1,0:T(8,128)(2,1)S(1)}, u32[]{:S(2)}, u32[]{:S(2)}) collective-permute-start(bf16[16,38912]{1,0:T(8,128)(2,1)S(1)} %collective-permute-done.8), channel_id=1, source_target_pairs={{0,2},{2,4},{4,6},{6,8},{8,10},{10,12},{12,14},{14,16},{16,18},{18... | collective-permute-start | bytes 3735560 | tf_op jit(solution)/shard_map/ppermute | solution.py:20
  208.3 1.1 copy-start.20
  209.3 19.0 %collective-permute-start.10 = (bf16[16,38912]{1,0:T(8,128)(2,1)S(1)}, bf16[16,38912]{1,0:T(8,128)(2,1)S(1)}, u32[]{:S(2)}, u32[]{:S(2)}) collective-permute-start(bf16[16,38912]{1,0:T(8,128)(2,1)S(1)} %collective-permute-done.9), channel_id=1, source_target_pairs={{0,2},{2,4},{4,6},{6,8},{8,10},{10,12},{12,14},{14,16},{16,18},{18... | collective-permute-start | bytes 3735560 | tf_op jit(solution)/shard_map/ppermute | solution.py:20
  228.4 1.0 copy-start.22
  229.4 19.0 %collective-permute-start.11 = (bf16[16,38912]{1,0:T(8,128)(2,1)S(1)}, bf16[16,38912]{1,0:T(8,128)(2,1)S(1)}, u32[]{:S(2)}, u32[]{:S(2)}) collective-permute-start(bf16[16,38912]{1,0:T(8,128)(2,1)S(1)} %collective-permute-done.10), channel_id=1, source_target_pairs={{0,2},{2,4},{4,6},{6,8},{8,10},{10,12},{12,14},{14,16},{16,18},{18... | collective-permute-start | bytes 3735560 | tf_op jit(solution)/shard_map/ppermute | solution.py:20
  248.4 1.0 copy-start.24
  249.5 19.0 %collective-permute-start.12 = (bf16[16,38912]{1,0:T(8,128)(2,1)S(1)}, bf16[16,38912]{1,0:T(8,128)(2,1)S(1)}, u32[]{:S(2)}, u32[]{:S(2)}) collective-permute-start(bf16[16,38912]{1,0:T(8,128)(2,1)S(1)} %collective-permute-done.11), channel_id=1, source_target_pairs={{0,2},{2,4},{4,6},{6,8},{8,10},{10,12},{12,14},{14,16},{16,18},{18... | collective-permute-start | bytes 3735560 | tf_op jit(solution)/shard_map/ppermute | solution.py:20
  268.5 1.0 copy-start.26
  269.5 19.1 %collective-permute-start.13 = (bf16[16,38912]{1,0:T(8,128)(2,1)S(1)}, bf16[16,38912]{1,0:T(8,128)(2,1)}, u32[]{:S(2)}, u32[]{:S(2)}) collective-permute-start(bf16[16,38912]{1,0:T(8,128)(2,1)S(1)} %collective-permute-done.12), channel_id=1, source_target_pairs={{0,2},{2,4},{4,6},{6,8},{8,10},{10,12},{12,14},{14,16},{16,18},{18... | collective-permute-start | bytes 3735560 | tf_op jit(solution)/shard_map/ppermute | solution.py:20
  288.7 19.3 %collective-permute-start.14 = (bf16[16,38912]{1,0:T(8,128)(2,1)}, bf16[16,38912]{1,0:T(8,128)(2,1)}, u32[]{:S(2)}, u32[]{:S(2)}) collective-permute-start(bf16[16,38912]{1,0:T(8,128)(2,1)} %collective-permute-done.13), channel_id=1, source_target_pairs={{0,2},{2,4},{4,6},{6,8},{8,10},{10,12},{12,14},{14,16},{16,18},{18... | collective-permute-start | bytes 3735560 | tf_op jit(solution)/shard_map/ppermute | solution.py:20
  290.0 46.0 %copy-start.1 = (bf16[16,38912]{1,0:T(8,128)(2,1)S(1)}, bf16[16,38912]{1,0:T(8,128)(2,1)}, u32[]{:S(2)}) copy-start(bf16[16,38912]{1,0:T(8,128)(2,1)} %param.10) | copy-start | bytes 3735556
  302.9 25.1 %copy-start.15 = (bf16[16,38912]{1,0:T(8,128)(2,1)S(1)}, bf16[16,38912]{1,0:T(8,128)(2,1)}, u32[]{:S(2)}) copy-start(bf16[16,38912]{1,0:T(8,128)(2,1)} %copy-done.14) | copy-start | bytes 3735556
  302.9 26.2 %copy-start.13 = (bf16[16,38912]{1,0:T(8,128)(2,1)S(1)}, bf16[16,38912]{1,0:T(8,128)(2,1)}, u32[]{:S(2)}) copy-start(bf16[16,38912]{1,0:T(8,128)(2,1)} %copy-done.12) | copy-start | bytes 3735556
  302.9 27.4 %copy-start.11 = (bf16[16,38912]{1,0:T(8,128)(2,1)S(1)}, bf16[16,38912]{1,0:T(8,128)(2,1)}, u32[]{:S(2)}) copy-start(bf16[16,38912]{1,0:T(8,128)(2,1)} %copy-done.10) | copy-start | bytes 3735556
  302.9 28.5 %copy-start.9 = (bf16[16,38912]{1,0:T(8,128)(2,1)S(1)}, bf16[16,38912]{1,0:T(8,128)(2,1)}, u32[]{:S(2)}) copy-start(bf16[16,38912]{1,0:T(8,128)(2,1)} %copy-done.8) | copy-start | bytes 3735556
  302.9 29.6 %copy-start.7 = (bf16[16,38912]{1,0:T(8,128)(2,1)S(1)}, bf16[16,38912]{1,0:T(8,128)(2,1)}, u32[]{:S(2)}) copy-start(bf16[16,38912]{1,0:T(8,128)(2,1)} %copy-done.6) | copy-start | bytes 3735556
  302.9 30.8 %copy-start.5 = (bf16[16,38912]{1,0:T(8,128)(2,1)S(1)}, bf16[16,38912]{1,0:T(8,128)(2,1)}, u32[]{:S(2)}) copy-start(bf16[16,38912]{1,0:T(8,128)(2,1)} %copy-done.4) | copy-start | bytes 3735556
  303.0 31.9 %copy-start.3 = (bf16[16,38912]{1,0:T(8,128)(2,1)S(1)}, bf16[16,38912]{1,0:T(8,128)(2,1)}, u32[]{:S(2)}) copy-start(bf16[16,38912]{1,0:T(8,128)(2,1)} %copy-done.2) | copy-start | bytes 3735556
  312.8 29.2 %copy-start.27 = (bf16[16,38912]{1,0:T(8,128)(2,1)S(1)}, bf16[16,38912]{1,0:T(8,128)(2,1)}, u32[]{:S(2)}) copy-start(bf16[16,38912]{1,0:T(8,128)(2,1)} %copy-done.26) | copy-start | bytes 3735556
  315.3 27.9 %copy-start.25 = (bf16[16,38912]{1,0:T(8,128)(2,1)S(1)}, bf16[16,38912]{1,0:T(8,128)(2,1)}, u32[]{:S(2)}) copy-start(bf16[16,38912]{1,0:T(8,128)(2,1)} %copy-done.24) | copy-start | bytes 3735556
  317.8 26.5 %copy-start.23 = (bf16[16,38912]{1,0:T(8,128)(2,1)S(1)}, bf16[16,38912]{1,0:T(8,128)(2,1)}, u32[]{:S(2)}) copy-start(bf16[16,38912]{1,0:T(8,128)(2,1)} %copy-done.22) | copy-start | bytes 3735556
  320.4 25.2 %copy-start.21 = (bf16[16,38912]{1,0:T(8,128)(2,1)S(1)}, bf16[16,38912]{1,0:T(8,128)(2,1)}, u32[]{:S(2)}) copy-start(bf16[16,38912]{1,0:T(8,128)(2,1)} %copy-done.20) | copy-start | bytes 3735556
  322.9 23.8 %copy-start.19 = (bf16[16,38912]{1,0:T(8,128)(2,1)S(1)}, bf16[16,38912]{1,0:T(8,128)(2,1)}, u32[]{:S(2)}) copy-start(bf16[16,38912]{1,0:T(8,128)(2,1)} %copy-done.18) | copy-start | bytes 3735556
  325.5 22.3 %copy-start.17 = (bf16[16,38912]{1,0:T(8,128)(2,1)S(1)}, bf16[16,38912]{1,0:T(8,128)(2,1)}, u32[]{:S(2)}) copy-start(bf16[16,38912]{1,0:T(8,128)(2,1)} %copy-done.16) | copy-start | bytes 3735556
  342.0 23.4 %copy-start.29 = (bf16[128,256]{1,0:T(8,128)(2,1)S(1)}, bf16[128,256]{1,0:T(8,128)(2,1)}, u32[]{:S(2)}) copy-start(bf16[128,256]{1,0:T(8,128)(2,1)} %all-reduce.2) | copy-start | bytes 196612
  406.2 28.2 %copy-start.28 = (bf16[128,4096]{1,0:T(8,128)(2,1)S(1)}, bf16[128,4096]{1,0:T(8,128)(2,1)}, u32[]{:S(2)}) copy-start(bf16[128,4096]{1,0:T(8,128)(2,1)} %param.8) | copy-start | bytes 3145732
  406.2 30.4 %copy-start.30 = (s32[128]{0:T(128)S(1)}, s32[128]{0:T(128)}, u32[]{:S(2)}) copy-start(s32[128]{0:T(128)} %param.15) | copy-start | bytes 1540
Sparse Core Ops, SparseCore 0:
  436.7 57.4 reduce-scatter.1
